TPU v7x, 32 devices: a whole 2x2x4 slice. The times are simulated.
32 devices in a mesh: group: 8 (over y, x, core), tensor: 4 (over z).
Axes of the slice: x: 2, y: 2, z: 4, core: 2. Of those that a mesh axis runs over, the one named last changes fastest.
Arguments:
- hidden: bfloat16 [768, 4096], P('group'), may hold values from -6 to 6
- query_weight: bfloat16 [4096, 4096], P(None, 'tensor'), may hold values from -0.09375 to 0.09375
- out_weight: bfloat16 [4096, 4096], P('tensor'), may hold values from -0.75 to 0.75
- prefix_keys: bfloat16 [9216, 16, 1024], P('group', None, 'tensor')
- prefix_values: bfloat16 [9216, 16, 1024], P('group', None, 'tensor'), may hold values from -6 to 6
- block_table: int32 [144, 64], P('group'), may hold values from 0 to 1151, as said below
- prompt_len: int32 [144], replicated, may hold values from 1 to 1024
- prompt_group: int32 [768], P('group'), may hold values from 0 to 143, as said below
- suffix_keys: bfloat16 [768, 128, 1024], P('group', None, 'tensor')
- suffix_values: bfloat16 [768, 128, 1024], P('group', None, 'tensor'), may hold values from -6 to 6
- suffix_len: int32 [768], P('group'), may hold values from 1 to 128
Outputs:
- attn_out: bfloat16 [768, 4096], P('group', 'tensor')
Inputs may be any that keep to these rules, and one draw needn't show every extreme that they name: `prompt_group`: each of the 144 prompt groups holds 4 to 8 requests, both sizes occurring; no two requests among one index of group's 96 requests share a prompt group. `block_table`: the 18 consecutive rows of one index of group list each of that index's 18 * 64 pool blocks exactly once.
All inputs are finite; a program needn't handle non-finite values.
Results may differ from a plain program's by a relative error of at most 0.0045.
The roundings to bfloat16 on the way count: a program that leaves them out, or rounds other values in their place, can miss the bound.
Values may be sent and summed in bfloat16 or wider, within the bound.
No kernel may reach another device: no remote copies, remote signals or barrier semaphores. Data moves between devices by JAX's collectives and lax.ppermute only.
A program may use at most 192 MiB of HBM per device.

v0:
```python
import math

import jax
import jax.numpy as jnp
from jax import lax
from jax.sharding import PartitionSpec as P

HD = 128


rope_base = 10000.0
masked_score = -1e30


def rotate(projected, position):
    half = projected.shape[-1] // 2
    freqs = rope_base ** (-(2.0 * jnp.arange(half, dtype=jnp.float32)) / projected.shape[-1])
    angles = position.astype(jnp.float32)[:, None, None] * freqs
    cosine = jnp.cos(angles)
    sine = jnp.sin(angles)
    former = projected[..., :half]
    latter = projected[..., half:]
    return jnp.concatenate(
        [former * cosine - latter * sine, latter * cosine + former * sine], axis=-1
    )


def softmax_parts(scores, valid_mask):
    masked = jnp.where(valid_mask, scores, masked_score)
    maximum = jnp.max(masked, axis=-1)
    weights = jnp.where(valid_mask, jnp.exp(masked - maximum[..., None]), 0.0)
    return (maximum, jnp.sum(weights, axis=-1), weights.astype(jnp.bfloat16))


def combine(far_peak, far_total, far_acc, near_peak, near_total, near_acc):
    highest = jnp.maximum(far_peak, near_peak)
    far_factor = jnp.exp(far_peak - highest)
    near_factor = jnp.exp(near_peak - highest)
    numer = far_acc * far_factor[..., None] + near_acc * near_factor[..., None]
    denom = far_total * far_factor + near_total * near_factor
    return numer / denom[..., None]


def body(
    hidden,
    query_weight,
    out_weight,
    prefix_keys,
    prefix_values,
    block_table,
    prompt_len,
    prompt_group,
    suffix_keys,
    suffix_values,
    suffix_len,
):
    groups = lax.axis_size("group")
    local_groups = block_table.shape[0]
    first_group = lax.axis_index("group") * local_groups
    requests = hidden.shape[0]
    kv_heads = prefix_keys.shape[2] // HD
    q_heads = query_weight.shape[1] // HD
    group_share = q_heads // kv_heads
    score_scale = 1.0 / math.sqrt(HD)
    projected = jnp.dot(hidden, query_weight, preferred_element_type=jnp.float32).reshape(
        requests, q_heads, HD
    )
    everyone = jnp.arange(prompt_len.shape[0], dtype=jnp.int32)
    own_prompt = jnp.sum(
        jnp.where(prompt_group[:, None] == everyone[None, :], prompt_len[None, :], 0), axis=1
    )
    position = own_prompt + suffix_len - 1
    rotated = rotate(projected, position).astype(jnp.bfloat16).reshape(requests, q_heads * HD)
    holder = prompt_group // local_groups
    slot_index = prompt_group % local_groups
    all_queries, all_groups = (
        lax.all_gather(rotated, "group", axis=0, tiled=True),
        lax.all_gather(prompt_group, "group", axis=0, tiled=True),
    )
    wanted = first_group + jnp.arange(local_groups, dtype=jnp.int32)
    picks = (all_groups.reshape(groups, requests)[:, :, None] == wanted[None, None, :]).astype(
        jnp.bfloat16
    )
    arrived = jnp.einsum(
        "srj,srq->sjq",
        picks,
        all_queries.reshape(groups, requests, q_heads * HD),
        preferred_element_type=jnp.float32,
    ).astype(jnp.bfloat16)
    far_queries = arrived.reshape(groups, local_groups, kv_heads, group_share, HD)
    far_keys = prefix_keys[block_table].reshape(local_groups, -1, kv_heads, HD)
    far_values = prefix_values[block_table].reshape(local_groups, -1, kv_heads, HD)
    key_count = far_keys.shape[1]
    my_lengths = lax.dynamic_slice_in_dim(prompt_len, first_group, local_groups)
    far_valid = jnp.arange(key_count, dtype=jnp.int32)[None, :] < my_lengths[:, None]
    far_scores = (
        jnp.einsum("sjkgd,jtkd->jkgst", far_queries, far_keys, preferred_element_type=jnp.float32)
        * score_scale
    )
    held_peak, held_total, held_weights = softmax_parts(
        far_scores, far_valid[:, None, None, None, :]
    )
    held_acc = jnp.einsum(
        "jkgst,jtkd->sjkgd", held_weights, far_values, preferred_element_type=jnp.float32
    )
    held_acc = held_acc.reshape(groups, local_groups, q_heads, HD)
    held_peak = jnp.transpose(held_peak, (3, 0, 1, 2)).reshape(groups, local_groups, q_heads)
    held_total = jnp.transpose(held_total, (3, 0, 1, 2)).reshape(groups, local_groups, q_heads)
    back_acc, back_peak, back_total = (
        lax.all_to_all(held_acc, "group", split_axis=0, concat_axis=0, tiled=True),
        lax.all_to_all(held_peak, "group", split_axis=0, concat_axis=0, tiled=True),
        lax.all_to_all(held_total, "group", split_axis=0, concat_axis=0, tiled=True),
    )
    far_acc = back_acc[holder, slot_index]
    far_peak = back_peak[holder, slot_index]
    far_total = back_total[holder, slot_index]
    near_queries = rotated.reshape(requests, kv_heads, group_share, HD)
    own_keys = suffix_keys.reshape(requests, -1, kv_heads, HD)
    own_values = suffix_values.reshape(requests, -1, kv_heads, HD)
    own_count = own_keys.shape[1]
    near_valid = jnp.arange(own_count, dtype=jnp.int32)[None, :] < suffix_len[:, None]
    near_scores = (
        jnp.einsum("rkgd,rtkd->rkgt", near_queries, own_keys, preferred_element_type=jnp.float32)
        * score_scale
    )
    near_peak, near_total, near_weights = softmax_parts(near_scores, near_valid[:, None, None, :])
    near_acc = jnp.einsum(
        "rkgt,rtkd->rkgd", near_weights, own_values, preferred_element_type=jnp.float32
    )
    near_acc = near_acc.reshape(requests, q_heads, HD)
    near_peak = near_peak.reshape(requests, q_heads)
    near_total = near_total.reshape(requests, q_heads)
    attn = combine(far_peak, far_total, far_acc, near_peak, near_total, near_acc)
    attn = attn.reshape(requests, q_heads * HD).astype(jnp.bfloat16)
    partial_out = jnp.dot(attn, out_weight, preferred_element_type=jnp.float32)
    return lax.psum_scatter(partial_out, "tensor", scatter_dimension=1, tiled=True).astype(
        jnp.bfloat16
    )


def solution(mesh):
    in_specs = (
        P("group", None),
        P(None, "tensor"),
        P("tensor", None),
        P("group", None, "tensor"),
        P("group", None, "tensor"),
        P("group", None),
        P(),
        P("group"),
        P("group", None, "tensor"),
        P("group", None, "tensor"),
        P("group"),
    )
    out_specs = P("group", "tensor")
    return jax.shard_map(body, mesh=mesh, in_specs=in_specs, out_specs=out_specs, check_vma=False)
```

profile of v0, /device:TPU:2, one launch (start us, length us, event | category | flops | bytes accessed | tf_op | source)
XLA Modules:
  0.0 178.4 jit_solution(6705385823124914175)
XLA Ops:
  6.6 1.1 copy-done
  7.7 4.9 %convolution_bitcast_fusion = f32[12,8,8,128]{3,1,2,0:T(8,128)S(1)} fusion(bf16[96,4096]{1,0:T(8,128)(2,1)S(1)} %copy-done, bf16[4096,1024]{1,0:T(8,128)(2,1)} %param.12), kind=kOutput, calls=%fused_computation.29 | convolution fusion | flops 805306368 | bytes 9568256 | tf_op jit(solution)/shard_map/dot_general | solution.py:65
  15.9 7.4 %all-reduce = s32[768]{0:T(1024)S(1)} all-reduce(s32[768]{0:T(1024)S(1)} %dynamic-update-slice), channel_id=1, replica_groups=mesh['group'=8,'tensor'=4] {'group'}, use_global_device_ids=true, to_apply=%add | all-reduce | flops 768 | bytes 6144
  23.4 9.8 %gather_fusion.1 = bf16[1152,16,256]{2,1,0:T(8,128)(2,1)} fusion(bf16[1152,16,256]{2,1,0:T(8,128)(2,1)} %param.14, s32[2048]{0:T(1024)S(1)} %pad_clamp_fusion), kind=kCustom, calls=%fused_computation.1 | custom fusion | bytes 18878976 | tf_op jit(solution)/shard_map/gather | solution.py:91
  33.2 14.1 %reshape.193 = bf16[18,1024,2,128]{3,2,1,0:T(2,128)(2,1)} reshape(bf16[1152,16,256]{2,1,0:T(8,128)(2,1)} %gather_fusion.1) | data formatting | bytes 18874368 | tf_op jit(solution)/shard_map/reshape | solution.py:91
  47.4 6.3 %fusion.57 = (f32[96,2,4]{2,1,0:T(2,128)S(1)}, f32[96,2,4,128]{3,2,1,0:T(4,128)S(1)}) fusion(bf16[96,2,4,64]{3,2,1,0:T(4,128)(2,1)S(1)} %bitcast.92, bf16[96,2,4,64]{3,2,1,0:T(4,128)(2,1)S(1)} %bitcast.91, pred[96,128]{1,0:T(8,128)(4,1)S(1)} %iota_compare_fusion.2, bf16[96,128,256]{2,1,0:T(8,128)(2,1)} %param.19), kind=kOutput, calls=%fused_computation.84 | convolution fusion | flops 25853184 | bytes 6896640 | tf_op jit(solution)/shard_map/rkgd,rtkd->rkgt/dot_general | solution.py:123
  53.8 1.8 convolution_convert_fusion
  55.7 6.7 %bitcast_reduce_fusion = (f32[18,2,4,8]{3,2,1,0:T(4,128)S(1)}, f32[18,2,1024,8,4]{2,3,4,1,0:T(8,128)S(1)}) fusion(pred[18,1024]{1,0:T(8,128)(4,1)S(1)} %iota_compare_fusion, bf16[8,18,2,4,128]{4,0,3,2,1:T(8,128)(2,1)S(1)} %bitcast.96, bf16[18,1024,2,128,1]{3,2,1,0,4:T(2,128)(2,1)} %bitcast.84), kind=kOutput, calls=%fused_computation.16 | convolution fusion | flops 305527680 | bytes 14473728 | tf_op jit(solution)/shard_map/sjkgd,jtkd->jkgst/dot_general | solution.py:97
  62.4 2.1 %copy-done.2 = f32[18,2,1024,8,4]{2,3,4,1,0:T(8,128)} copy-done((f32[18,2,1024,8,4]{2,3,4,1,0:T(8,128)}, f32[18,2,1024,8,4]{2,3,4,1,0:T(8,128)S(1)}, u32[]{:S(2)}) %copy-start.2) | copy-done | bytes 4718616
  64.6 1.6 fusion.12
  67.0 4.3 %all-to-all-start.2 = ((f32[8,1,144]{2,1,0:T(1,128)}), f32[8,1,144]{2,1,0:T(1,128)S(1)}, u32[]{:S(2)}, u32[]{:S(2)}) async-start(f32[8,1,144]{2,1,0:T(1,128)} %reshape.266), calls=%async_computation.2 | async-start | bytes 16384 | tf_op jit(solution)/shard_map/all_to_all | solution.py:112
  71.4 4.6 %fusion.4 = f32[96,2,4,128]{3,2,1,0:T(4,128)S(1)} fusion(f32[96,2,4,128]{3,2,1,0:T(4,128)S(1)} %get-tuple-element.13, f32[96,2,4]{2,1,0:T(2,128)S(1)} %get-tuple-element.12, pred[96,128]{1,0:T(8,128)(4,1)S(1)} %iota_compare_fusion.2, bf16[96,128,256]{2,1,0:T(8,128)(2,1)} %param.20), kind=kOutput, calls=%fused_computation.9 | convolution fusion | flops 25460736 | bytes 7093248 | tf_op jit(solution)/shard_map/rkgt,rtkd->rkgd/dot_general | solution.py:127
  75.9 9.7 %gather_fusion = bf16[1152,16,256]{2,1,0:T(8,128)(2,1)} fusion(bf16[1152,16,256]{2,1,0:T(8,128)(2,1)} %param.15, s32[2048]{0:T(1024)S(1)} %pad_clamp_fusion), kind=kCustom, calls=%fused_computation | custom fusion | bytes 18878976 | tf_op jit(solution)/shard_map/gather | solution.py:92
  85.7 14.0 %reshape.192 = bf16[18,1024,2,128]{3,2,1,0:T(2,128)(2,1)} reshape(bf16[1152,16,256]{2,1,0:T(8,128)(2,1)} %gather_fusion) | data formatting | bytes 18874368 | tf_op jit(solution)/shard_map/reshape | solution.py:92
  100.5 4.2 %all-to-all-start.1 = ((f32[8,1,144]{2,1,0:T(1,128)}), f32[8,1,144]{2,1,0:T(1,128)S(1)}, u32[]{:S(2)}, u32[]{:S(2)}) async-start(f32[8,1,144]{2,1,0:T(1,128)} %reshape.264), calls=%async_computation.1 | async-start | bytes 16384 | tf_op jit(solution)/shard_map/all_to_all | solution.py:111
  104.7 7.5 %fusion.2 = f32[18,2,128,4,8]{2,4,3,1,0:T(8,128)S(1)} fusion(bf16[18,1024,2,128,1]{3,2,1,0,4:T(2,128)(2,1)} %bitcast.85, f32[18,2,1024,8,4]{2,3,4,1,0:T(8,128)} %copy-done.2, f32[18,2,4,8]{3,2,1,0:T(4,128)S(1)} %get-tuple-element.14, pred[18,1024]{1,0:T(8,128)(4,1)S(1)} %iota_compare_fusion), kind=kOutput, calls=%fused_computation.7 | convolution fusion | flops 307888128 | bytes 14768640 | tf_op jit(solution)/shard_map/jkgst,jtkd->sjkgd/dot_general | solution.py:103
  113.1 4.2 %all-to-all-start = ((f32[8,18,8,128]{3,2,1,0:T(8,128)}), f32[8,18,8,128]{3,2,1,0:T(8,128)S(1)}, u32[]{:S(2)}, u32[]{:S(2)}) async-start(f32[8,18,8,128]{3,2,1,0:T(8,128)} %copy.69), calls=%async_computation | async-start | bytes 1179648 | tf_op jit(solution)/shard_map/all_to_all | solution.py:110
  119.7 1.1 gather_fusion.4
  121.7 1.1 gather_fusion.3
  123.2 3.1 %all-to-all-done = f32[8,18,8,128]{3,2,1,0:T(8,128)S(1)} async-done(((f32[8,18,8,128]{3,2,1,0:T(8,128)}), f32[8,18,8,128]{3,2,1,0:T(8,128)S(1)}, u32[]{:S(2)}, u32[]{:S(2)}) %all-to-all-start) | async-done | bytes 589856 | tf_op jit(solution)/shard_map/all_to_all | solution.py:110
  126.3 1.1 gather_fusion.2
  127.9 6.2 %fusion.32 = f32[96,4096]{1,0:T(8,128)} fusion(bf16[1024,4096]{1,0:T(8,128)(2,1)} %param.13, f32[12,8,8,128]{3,2,1,0:T(8,128)S(1)} %bitcast.89, f32[96,1024]{1,0:T(8,128)S(1)} %reshape.202, f32[12,8,8,128]{3,2,1,0:T(8,128)S(1)} %bitcast.88, f32[12,8,8,128]{3,2,1,0:T(8,128)S(1)} %bitcast.87), kind=kOutput, calls=%fused_computation.41 | convolution fusion | flops 805699584 | bytes 11534336 | tf_op jit(solution)/shard_map/dot_general | solution.py:135
  134.1 35.7 %reduce-scatter.2.cloned.1.call-done = f32[96,1024]{1,0:T(8,128)} async-done(((f32[96,4096]{1,0:T(8,128)}), f32[96,1024]{1,0:T(8,128)}) %reduce-scatter.2.cloned.1.call-update) | async-done | bytes 393232 | tf_op jit(solution)/shard_map/reduce_scatter | solution.py:136
  169.8 1.7 convert_element_type.31
  (67 shorter events, 9.8 us)
Async XLA Ops:
  6.5 1.1 copy-start
  6.5 47.2 %all-gather.2.cloned.1.call-start = ((), (), s32[]{:S(2)}) async-start(), calls=%async_computation.4 | async-start | bytes 1769472 | tf_op jit(solution)/shard_map/all_gather | solution.py:77
  7.7 5.0 %copy-start.4 = (s32[144]{0:T(256)S(1)}, s32[144]{0:T(256)}, u32[]{:S(2)}) copy-start(s32[144]{0:T(256)} %param.17) | copy-start | bytes 1732
  7.7 5.0 %copy-start.6 = (s32[96]{0:T(128)S(1)}, s32[96]{0:T(128)}, u32[]{:S(2)}) copy-start(s32[96]{0:T(128)} %param.18) | copy-start | bytes 1156
  7.7 5.1 %copy-start.5 = (s32[96]{0:T(128)S(1)}, s32[96]{0:T(128)}, u32[]{:S(2)}) copy-start(s32[96]{0:T(128)} %param.21) | copy-start | bytes 1156
  7.7 6.6 %copy-start.7 = (u32[32]{0:T(128)S(1)}, u32[32]{0:T(128)}, u32[]{:S(2)}) copy-start(u32[32]{0:T(128)} %constant.96) | copy-start | bytes 388
  7.7 15.6 %copy-start.3 = (s32[18,64]{1,0:T(8,128)S(1)}, s32[18,64]{1,0:T(8,128)}, u32[]{:S(2)}) copy-start(s32[18,64]{1,0:T(8,128)} %param.16) | copy-start | bytes 13828
  62.4 2.2 %copy-start.2 = (f32[18,2,1024,8,4]{2,3,4,1,0:T(8,128)}, f32[18,2,1024,8,4]{2,3,4,1,0:T(8,128)S(1)}, u32[]{:S(2)}) copy-start(f32[18,2,1024,8,4]{2,3,4,1,0:T(8,128)S(1)} %get-tuple-element.15) | copy-start | bytes 14155780
  67.0 33.4 %all-to-all-start.2 = ((f32[8,1,144]{2,1,0:T(1,128)}), f32[8,1,144]{2,1,0:T(1,128)S(1)}, u32[]{:S(2)}, u32[]{:S(2)}) async-start(f32[8,1,144]{2,1,0:T(1,128)} %reshape.266), calls=%async_computation.2 | async-start | bytes 16384 | tf_op jit(solution)/shard_map/all_to_all | solution.py:112
  100.5 12.6 %all-to-all-start.1 = ((f32[8,1,144]{2,1,0:T(1,128)}), f32[8,1,144]{2,1,0:T(1,128)S(1)}, u32[]{:S(2)}, u32[]{:S(2)}) async-start(f32[8,1,144]{2,1,0:T(1,128)} %reshape.264), calls=%async_computation.1 | async-start | bytes 16384 | tf_op jit(solution)/shard_map/all_to_all | solution.py:111
  113.1 13.2 %all-to-all-start = ((f32[8,18,8,128]{3,2,1,0:T(8,128)}), f32[8,18,8,128]{3,2,1,0:T(8,128)S(1)}, u32[]{:S(2)}, u32[]{:S(2)}) async-start(f32[8,18,8,128]{3,2,1,0:T(8,128)} %copy.69), calls=%async_computation | async-start | bytes 1179648 | tf_op jit(solution)/shard_map/all_to_all | solution.py:110
  117.3 52.5 %reduce-scatter.2.cloned.1.call-start = ((), (), s32[]{:S(2)}) async-start(), calls=%async_computation.5 | async-start | bytes 1966080 | tf_op jit(solution)/shard_map/reduce_scatter | solution.py:136
  127.9 43.6 %copy-start.1 = (bf16[96,4096]{1,0:T(8,128)(2,1)S(1)}, bf16[96,4096]{1,0:T(8,128)(2,1)}, u32[]{:S(2)}) copy-start(bf16[96,4096]{1,0:T(8,128)(2,1)} %param.11) | copy-start | bytes 2359300
Sparse Core Ops, SparseCore 0:
  14.3 26.9 all-gather.1
  134.2 35.5 reduce-scatter.1
where the time goes:
time: 181 us; the launch traced here: 178 us
  local copies, waits for them, and re-layouts  60.8 us (34%)
  waiting for transfers between devices  38.8 us (21%)
  matrix products  37.9 us (21%)
  between operations  14.3 us (8%)
  starting transfers between devices  12.7 us (7%)
  blocking collectives  7.38 us (4%)
  other arithmetic  6.39 us (4%)
    reduce_scatter x1, waiting for transfers between devices, body(): lax.psum_scatter(partial_out, 'tensor', scatter_dimension=1, tiled=True)  35.7 us
    reshape x1, local copies, waits for them, and re-layouts, body(): far_keys = prefix_keys[block_table].reshape(local_groups, -1, kv_heads, HD)  14.1 us
    reshape x1, local copies, waits for them, and re-layouts, body(): prefix_values[block_table].reshape(local_groups, -1, kv_heads, HD)  14 us
    gather x1, local copies, waits for them, and re-layouts, body(): far_keys = prefix_keys[block_table].reshape(local_groups, -1, kv_heads, HD)  9.75 us
    gather x1, local copies, waits for them, and re-layouts, body(): prefix_values[block_table].reshape(local_groups, -1, kv_heads, HD)  9.74 us
    dot_general x1, matrix products, body(): jnp.einsum('jkgst,jtkd->sjkgd', held_weights, far_values, preferred_eleme...  7.45 us
    unnamed x1, blocking collectives  7.38 us
    dot_general x1, matrix products, body(): jnp.einsum('sjkgd,jtkd->jkgst', far_queries, far_keys, preferred_element_...  6.69 us
  transfers between devices with their start and end apart: 5, of which 2 were waited for; matrix products, arithmetic and copies ran while one was open for 42% of the time, Pallas kernels for 0%

commit v1 on v0

v1 whole, which is shorter than its diff:
```python
import math

import jax
import jax.numpy as jnp
from jax import lax
from jax.sharding import PartitionSpec as P

HD = 128


rope_base = 10000.0
masked_score = -1e30


def rotate(projected, position):
    half = projected.shape[-1] // 2
    freqs = rope_base ** (-(2.0 * jnp.arange(half, dtype=jnp.float32)) / projected.shape[-1])
    angles = position.astype(jnp.float32)[:, None, None] * freqs
    cosine = jnp.cos(angles)
    sine = jnp.sin(angles)
    former = projected[..., :half]
    latter = projected[..., half:]
    return jnp.concatenate(
        [former * cosine - latter * sine, latter * cosine + former * sine], axis=-1
    )


def softmax_parts(scores, valid_mask):
    masked = jnp.where(valid_mask, scores, masked_score)
    maximum = jnp.max(masked, axis=-1)
    weights = jnp.where(valid_mask, jnp.exp(masked - maximum[..., None]), 0.0)
    return (maximum, jnp.sum(weights, axis=-1), weights.astype(jnp.bfloat16))


def combine(far_peak, far_total, far_acc, near_peak, near_total, near_acc):
    highest = jnp.maximum(far_peak, near_peak)
    far_factor = jnp.exp(far_peak - highest)
    near_factor = jnp.exp(near_peak - highest)
    numer = far_acc * far_factor[..., None] + near_acc * near_factor[..., None]
    denom = far_total * far_factor + near_total * near_factor
    return numer / denom[..., None]


def spread_lanes(queries, kv_heads):
    lead = queries.shape[:-3]
    share = queries.shape[-2]
    eye = (jnp.arange(kv_heads)[:, None] == jnp.arange(kv_heads)[None, :]).astype(queries.dtype)
    eye = eye.reshape((1,) * len(lead) + (kv_heads, 1, kv_heads, 1))
    wide = queries[..., None, :] * eye
    return wide.reshape(lead + (kv_heads * share, kv_heads * HD))


def pick_lanes(wide, kv_heads):
    lead = wide.shape[:-2]
    share = wide.shape[-2] // kv_heads
    w = wide.reshape(lead + (kv_heads, share, kv_heads, HD))
    return jnp.stack([w[..., k, :, k, :] for k in range(kv_heads)], axis=-3)


def body(
    hidden,
    query_weight,
    out_weight,
    prefix_keys,
    prefix_values,
    block_table,
    prompt_len,
    prompt_group,
    suffix_keys,
    suffix_values,
    suffix_len,
):
    groups = lax.axis_size("group")
    local_groups = block_table.shape[0]
    first_group = lax.axis_index("group") * local_groups
    requests = hidden.shape[0]
    width = prefix_keys.shape[2]
    kv_heads = width // HD
    q_heads = query_weight.shape[1] // HD
    share = q_heads // kv_heads
    score_scale = 1.0 / math.sqrt(HD)

    projected = jnp.dot(hidden, query_weight, preferred_element_type=jnp.float32).reshape(
        requests, q_heads, HD
    )
    position = prompt_len[prompt_group] + suffix_len - 1
    rotated = rotate(projected, position).astype(jnp.bfloat16)

    slots = jnp.arange(groups * local_groups, dtype=jnp.int32)
    picks = (slots[:, None] == prompt_group[None, :]).astype(jnp.bfloat16)
    outgoing = jnp.dot(
        picks, rotated.reshape(requests, q_heads * HD), preferred_element_type=jnp.float32
    ).astype(jnp.bfloat16)
    arrived = lax.all_to_all(
        outgoing.reshape(groups, local_groups, q_heads * HD),
        "group",
        split_axis=0,
        concat_axis=0,
        tiled=True,
    )
    far_queries = jnp.transpose(
        arrived.reshape(groups, local_groups, kv_heads, share, HD), (1, 0, 2, 3, 4)
    )
    far_queries = spread_lanes(far_queries, kv_heads).reshape(
        local_groups, groups * q_heads, width
    )
    far_keys = prefix_keys[block_table].reshape(local_groups, -1, width)
    far_values = prefix_values[block_table].reshape(local_groups, -1, width)
    key_count = far_keys.shape[1]
    my_lengths = lax.dynamic_slice_in_dim(prompt_len, first_group, local_groups)
    far_valid = jnp.arange(key_count, dtype=jnp.int32)[None, None, :] < my_lengths[:, None, None]
    far_scores = (
        jnp.einsum("jqc,jtc->jqt", far_queries, far_keys, preferred_element_type=jnp.float32)
        * score_scale
    )
    held_peak, held_total, held_weights = softmax_parts(far_scores, far_valid)
    held_wide = jnp.einsum(
        "jqt,jtc->jqc", held_weights, far_values, preferred_element_type=jnp.float32
    )
    held_acc = pick_lanes(held_wide.reshape(local_groups, groups, q_heads, width), kv_heads)
    held_acc = jnp.transpose(
        held_acc.reshape(local_groups, groups, q_heads, HD), (1, 0, 2, 3)
    )
    stats = jnp.concatenate(
        [
            held_peak.reshape(local_groups, groups, q_heads),
            held_total.reshape(local_groups, groups, q_heads),
            jnp.zeros((local_groups, groups, HD - 2 * q_heads), jnp.float32),
        ],
        axis=-1,
    )
    stats = jnp.transpose(stats, (1, 0, 2))[:, :, None, :]
    packed = jnp.concatenate([held_acc, stats], axis=2)
    back = lax.all_to_all(packed, "group", split_axis=0, concat_axis=0, tiled=True)
    holder = prompt_group // local_groups
    slot_index = prompt_group % local_groups
    mine = back[holder, slot_index]
    far_acc = mine[:, :q_heads, :]
    far_peak = mine[:, q_heads, :q_heads]
    far_total = mine[:, q_heads, q_heads : 2 * q_heads]

    near_queries = spread_lanes(rotated.reshape(requests, kv_heads, share, HD), kv_heads)
    own_count = suffix_keys.shape[1]
    near_valid = jnp.arange(own_count, dtype=jnp.int32)[None, None, :] < suffix_len[:, None, None]
    near_scores = (
        jnp.einsum("rqc,rtc->rqt", near_queries, suffix_keys, preferred_element_type=jnp.float32)
        * score_scale
    )
    near_peak, near_total, near_weights = softmax_parts(near_scores, near_valid)
    near_wide = jnp.einsum(
        "rqt,rtc->rqc", near_weights, suffix_values, preferred_element_type=jnp.float32
    )
    near_acc = pick_lanes(near_wide, kv_heads).reshape(requests, q_heads, HD)
    attn = combine(far_peak, far_total, far_acc, near_peak, near_total, near_acc)
    attn = attn.reshape(requests, q_heads * HD).astype(jnp.bfloat16)
    partial_out = jnp.dot(attn, out_weight, preferred_element_type=jnp.float32)
    return lax.psum_scatter(partial_out, "tensor", scatter_dimension=1, tiled=True).astype(
        jnp.bfloat16
    )


def solution(mesh):
    in_specs = (
        P("group", None),
        P(None, "tensor"),
        P("tensor", None),
        P("group", None, "tensor"),
        P("group", None, "tensor"),
        P("group", None),
        P(),
        P("group"),
        P("group", None, "tensor"),
        P("group", None, "tensor"),
        P("group"),
    )
    out_specs = P("group", "tensor")
    return jax.shard_map(body, mesh=mesh, in_specs=in_specs, out_specs=out_specs, check_vma=False)
```

time: 181 us -> 138 us (0.76)
  local copies, waits for them, and re-layouts: 60.8 us -> 29.1 us
  blocking collectives: 7.38 us -> 0 us
  matrix products: 37.9 us -> 33.1 us
  starting transfers between devices: 12.7 us -> 8.46 us
  waiting for transfers between devices: 38.8 us -> 43 us
  other arithmetic: 6.39 us -> 8.47 us
    reshape x6 -> x4, local copies, waits for them, and re-layouts: 29.4 us -> 1.5 us  [the longest x1 0.84 us: body(): outgoing.reshape(groups, local_groups, q_heads * HD)]
    unnamed x1 -> x0, blocking collectives: 7.38 us -> none
    unnamed x25 -> x17, local copies, waits for them, and re-layouts: 6.52 us -> 0.49 us
    dot_general x5, matrix products: 26.8 us -> 22.2 us  [the longest x1 8.84 us: body(): jnp.einsum('jqc,jtc->jqt', far_queries, far_keys, preferred_element_type=...]
    all_to_all x3 -> x2, starting transfers between devices: 12.7 us -> 8.46 us  [the longest x1 4.26 us: body(): lax.all_to_all(outgoing.reshape(groups, local_groups, q_heads * HD), 'gro...]
    all_to_all x3 -> x2, waiting for transfers between devices: 3.06 us -> 7.14 us  [the longest x1 7.14 us: body(): lax.all_to_all(packed, 'group', split_axis=0, concat_axis=0, tiled=True)]
    reduce_sum x2, other arithmetic: 2.24 us -> 4.28 us  [softmax_parts(): return (maximum, jnp.sum(weights, axis=-1), weights.astype(jnp.bfloat16))]
    gather x7 -> x4, local copies, waits for them, and re-layouts: 22.9 us -> 21.8 us  [the longest x1 9.73 us: body(): far_keys = prefix_keys[block_table].reshape(local_groups, -1, width)]
  transfers between devices with their start and end apart: 5 -> 3, of which waited for: 2 -> 2; matrix products, arithmetic and copies ran while one was open for 42% -> 22% of each run, Pallas kernels for 0% -> 0%
where the time goes in v1:
time: 138 us; the launch traced here: 136 us
  waiting for transfers between devices  43 us (31%)
  matrix products  33.1 us (24%)
  local copies, waits for them, and re-layouts  29.1 us (21%)
  between operations  13.7 us (10%)
  other arithmetic  8.47 us (6%)
  starting transfers between devices  8.46 us (6%)
    reduce_scatter x1, waiting for transfers between devices, body(): lax.psum_scatter(partial_out, 'tensor', scatter_dimension=1, tiled=True)  35.8 us
    gather x1, local copies, waits for them, and re-layouts, body(): far_keys = prefix_keys[block_table].reshape(local_groups, -1, width)  9.73 us
    gather x1, local copies, waits for them, and re-layouts, body(): far_values = prefix_values[block_table].reshape(local_groups, -1, width)  9.69 us
    dot_general x1, matrix products, body(): jnp.einsum('jqc,jtc->jqt', far_queries, far_keys, preferred_element_type=...  8.84 us
    all_to_all x1, waiting for transfers between devices, body(): lax.all_to_all(packed, 'group', split_axis=0, concat_axis=0, tiled=True)  7.14 us
    dot_general x1, matrix products, body(): partial_out = jnp.dot(attn, out_weight, preferred_element_type=jnp.float32)  6.06 us
    dot_general x1, matrix products, body(): jnp.dot(hidden, query_weight, preferred_element_type=jnp.float32)  4.87 us
    dot_general x1, matrix products, body(): jnp.einsum('jqt,jtc->jqc', held_weights, far_values, preferred_element_ty...  4.8 us
  transfers between devices with their start and end apart: 3, of which 2 were waited for; matrix products, arithmetic and copies ran while one was open for 22% of the time, Pallas kernels for 0%

profile of v1, /device:TPU:2, one launch (start us, length us, event | category | flops | bytes accessed | tf_op | source)
XLA Modules:
  0.0 135.8 jit_solution(8764340364847182771)
XLA Ops:
  6.5 0.7 fusion.36
  7.7 4.9 %convolution_bitcast_fusion = f32[12,8,8,128]{3,1,2,0:T(8,128)S(1)} fusion(bf16[96,4096]{1,0:T(8,128)(2,1)S(1)} %copy-done, bf16[4096,1024]{1,0:T(8,128)(2,1)} %param.12), kind=kOutput, calls=%fused_computation.18 | convolution fusion | flops 805306368 | bytes 9568256 | tf_op jit(solution)/shard_map/dot_general | solution.py:83
  12.7 1.3 gather_fusion
  14.8 0.8 reshape.230
  15.7 4.3 %all-to-all-start = ((bf16[8,18,1024]{2,1,0:T(8,128)(2,1)}), bf16[8,18,1024]{2,1,0:T(8,128)(2,1)S(1)}, u32[]{:S(2)}, u32[]{:S(2)}) async-start(bf16[8,18,1024]{2,1,0:T(8,128)(2,1)} %reshape.230), calls=%async_computation | async-start | bytes 786432 | tf_op jit(solution)/shard_map/all_to_all | solution.py:94
  21.0 4.6 %fusion.48 = (f32[96,8]{1,0:T(8,128)S(1)}, f32[96,8,128]{2,1,0:T(8,128)S(1)}) fusion(bf16[96,128,256]{2,1,0:T(8,128)(2,1)} %param.19, bf16[96,8,256]{2,1,0:T(8,128)(2,1)S(1)} %mul.165, bf16[8,256]{1,0:T(8,128)(2,1)S(1)} %bitcast.75, pred[96,128]{1,0:T(8,128)(4,1)S(1)} %iota_compare_fusion.3), kind=kOutput, calls=%fused_computation.86 | convolution fusion | flops 50822400 | bytes 7097344 | tf_op jit(solution)/shard_map/rqc,rtc->rqt/dot_general | solution.py:146
  25.8 9.7 %gather_fusion.1 = bf16[1152,16,256]{2,1,0:T(8,128)(2,1)} fusion(bf16[1152,16,256]{2,1,0:T(8,128)(2,1)} %param.14, s32[2048]{0:T(1024)S(1)} %pad_clamp_fusion), kind=kCustom, calls=%fused_computation.1 | custom fusion | bytes 18878976 | tf_op jit(solution)/shard_map/gather | solution.py:107
  35.5 9.7 %gather_fusion.2 = bf16[1152,16,256]{2,1,0:T(8,128)(2,1)} fusion(bf16[1152,16,256]{2,1,0:T(8,128)(2,1)} %param.15, s32[2048]{0:T(1024)S(1)} %pad_clamp_fusion), kind=kCustom, calls=%fused_computation.2 | custom fusion | bytes 18878976 | tf_op jit(solution)/shard_map/gather | solution.py:108
  45.7 0.5 mul.156
  46.2 0.4 mul.157
  46.6 8.8 %fusion = (f32[18,64]{1,0:T(8,128)S(1)}, f32[18,64,1024]{2,1,0:T(8,128)}) fusion(pred[18,1024]{1,0:T(8,128)(4,1)S(1)} %iota_compare_fusion, bf16[18,1024,256]{2,1,0:T(8,128)(2,1)} %bitcast.57, bf16[18,64,256]{2,1,0:T(8,128)(2,1)S(1)} %mul.157, bf16[64,256]{1,0:T(8,128)(2,1)S(1)} %bitcast.71), kind=kOutput, calls=%fused_computation.6 | convolution fusion | flops 607812480 | bytes 14801408 | tf_op jit(solution)/shard_map/jqc,jtc->jqt/dot_general | solution.py:113
  55.5 4.0 %fusion.1 = f32[18,64]{1,0:T(8,128)S(1)} fusion(f32[18,64,1024]{2,1,0:T(8,128)} %get-tuple-element.23, f32[18,64]{1,0:T(8,128)S(1)} %get-tuple-element.22, pred[18,1024]{1,0:T(8,128)(4,1)S(1)} %iota_compare_fusion), kind=kLoop, calls=%fused_computation.7 | loop fusion | flops 5897088 | bytes 4746240 | tf_op jit(solution)/shard_map/reduce_sum | solution.py:32
  59.5 4.8 %fusion.3 = f32[18,64,256]{2,1,0:T(8,128)S(1)} fusion(bf16[18,1024,256]{2,1,0:T(8,128)(2,1)} %bitcast.58, f32[18,64,1024]{2,1,0:T(8,128)S(1)} %copy-done.3, f32[18,64]{1,0:T(8,128)S(1)} %get-tuple-element.22, pred[18,1024]{1,0:T(8,128)(4,1)S(1)} %iota_compare_fusion), kind=kOutput, calls=%fused_computation.9 | convolution fusion | flops 609878016 | bytes 15358464 | tf_op jit(solution)/shard_map/jqt,jtc->jqc/dot_general | solution.py:117
  64.3 0.6 reshape_reshape.4
  64.9 0.5 fusion.45
  66.0 1.1 copy.50
  67.1 4.2 %all-to-all-start.1 = ((f32[8,18,9,128]{3,1,2,0:T(8,128)}), f32[8,18,9,128]{3,1,2,0:T(8,128)S(1)}, u32[]{:S(2)}, u32[]{:S(2)}) async-start(f32[8,18,9,128]{3,1,2,0:T(8,128)} %copy.50), calls=%async_computation.1 | async-start | bytes 1769472 | tf_op jit(solution)/shard_map/all_to_all | solution.py:134
  71.3 3.8 %fusion.20 = f32[96,8,256]{2,1,0:T(8,128)S(1)} fusion(bf16[96,128,256]{2,1,0:T(8,128)(2,1)} %param.20, f32[96,8,128]{2,1,0:T(8,128)S(1)} %get-tuple-element.21, f32[96,8]{1,0:T(8,128)S(1)} %get-tuple-element.20, pred[96,128]{1,0:T(8,128)(4,1)S(1)} %iota_compare_fusion.3), kind=kOutput, calls=%fused_computation.37 | convolution fusion | flops 50626560 | bytes 7486464 | tf_op jit(solution)/shard_map/rqt,rtc->rqc/dot_general | solution.py:150
  75.1 0.4 reshape.237
  76.3 7.1 %all-to-all-done.1 = f32[8,18,9,128]{3,1,2,0:T(8,128)S(1)} async-done(((f32[8,18,9,128]{3,1,2,0:T(8,128)}), f32[8,18,9,128]{3,1,2,0:T(8,128)S(1)}, u32[]{:S(2)}, u32[]{:S(2)}) %all-to-all-start.1) | async-done | bytes 663584 | tf_op jit(solution)/shard_map/all_to_all | solution.py:134
  83.6 1.2 gather_fusion.3
  85.4 6.1 %fusion.22 = f32[96,4096]{1,0:T(8,128)} fusion(bf16[1024,4096]{1,0:T(8,128)(2,1)} %param.13, bf16[12,8,8,128]{3,2,1,0:T(8,128)(2,1)S(1)} %bitcast.64), kind=kOutput, calls=%fused_computation.38 | convolution fusion | flops 805306368 | bytes 10158080 | tf_op jit(solution)/shard_map/dot_general | solution.py:156
  91.5 35.8 %reduce-scatter.2.cloned.1.call-done = f32[96,1024]{1,0:T(8,128)} async-done(((f32[96,4096]{1,0:T(8,128)}), f32[96,1024]{1,0:T(8,128)}) %reduce-scatter.2.cloned.1.call-update) | async-done | bytes 393232 | tf_op jit(solution)/shard_map/reduce_scatter | solution.py:157
  127.3 1.7 %convert_element_type.53 = bf16[96,1024]{1,0:T(8,128)(2,1)} convert(f32[96,1024]{1,0:T(8,128)} %reduce-scatter.2.cloned.1.call-done) | non-fusion elementwise | flops 98304 | bytes 589824 | tf_op jit(solution)/shard_map/convert_element_type | solution.py:157
  (59 shorter events, 5.2 us)
Async XLA Ops:
  6.5 1.1 copy-start
  7.7 5.0 %copy-start.2 = (s32[144]{0:T(256)S(1)}, s32[144]{0:T(256)}, u32[]{:S(2)}) copy-start(s32[144]{0:T(256)} %param.17) | copy-start | bytes 1732
  7.7 6.3 %copy-start.6 = (s32[96]{0:T(128)S(1)}, s32[96]{0:T(128)}, u32[]{:S(2)}) copy-start(s32[96]{0:T(128)} %param.21) | copy-start | bytes 1156
  7.7 6.9 %copy-start.5 = (s32[96]{0:T(128)S(1)}, s32[96]{0:T(128)}, u32[]{:S(2)}) copy-start(s32[96]{0:T(128)} %param.18) | copy-start | bytes 1156
  12.6 7.4 %copy-start.4 = (s32[18,64]{1,0:T(8,128)S(1)}, s32[18,64]{1,0:T(8,128)}, u32[]{:S(2)}) copy-start(s32[18,64]{1,0:T(8,128)} %param.16) | copy-start | bytes 13828
  15.7 29.7 %all-to-all-start = ((bf16[8,18,1024]{2,1,0:T(8,128)(2,1)}), bf16[8,18,1024]{2,1,0:T(8,128)(2,1)S(1)}, u32[]{:S(2)}, u32[]{:S(2)}) async-start(bf16[8,18,1024]{2,1,0:T(8,128)(2,1)} %reshape.230), calls=%async_computation | async-start | bytes 786432 | tf_op jit(solution)/shard_map/all_to_all | solution.py:94
  55.5 4.0 %copy-start.3 = (f32[18,64,1024]{2,1,0:T(8,128)S(1)}, f32[18,64,1024]{2,1,0:T(8,128)}, u32[]{:S(2)}) copy-start(f32[18,64,1024]{2,1,0:T(8,128)} %get-tuple-element.23) | copy-start | bytes 14155780
  67.1 16.4 %all-to-all-start.1 = ((f32[8,18,9,128]{3,1,2,0:T(8,128)}), f32[8,18,9,128]{3,1,2,0:T(8,128)S(1)}, u32[]{:S(2)}, u32[]{:S(2)}) async-start(f32[8,18,9,128]{3,1,2,0:T(8,128)} %copy.50), calls=%async_computation.1 | async-start | bytes 1769472 | tf_op jit(solution)/shard_map/all_to_all | solution.py:134
  71.3 56.0 %reduce-scatter.2.cloned.1.call-start = ((), (), s32[]{:S(2)}) async-start(), calls=%async_computation.3 | async-start | bytes 1966080 | tf_op jit(solution)/shard_map/reduce_scatter | solution.py:157
  85.4 43.6 %copy-start.1 = (bf16[96,4096]{1,0:T(8,128)(2,1)S(1)}, bf16[96,4096]{1,0:T(8,128)(2,1)}, u32[]{:S(2)}) copy-start(bf16[96,4096]{1,0:T(8,128)(2,1)} %param.11) | copy-start | bytes 2359300
Sparse Core Ops, SparseCore 0:
  91.6 35.6 reduce-scatter.1

commit v2 on v1

--- a/solution.py
+++ b/solution.py
@@ -154,9 +154,11 @@
     attn = combine(far_peak, far_total, far_acc, near_peak, near_total, near_acc)
     attn = attn.reshape(requests, q_heads * HD).astype(jnp.bfloat16)
     partial_out = jnp.dot(attn, out_weight, preferred_element_type=jnp.float32)
-    return lax.psum_scatter(partial_out, "tensor", scatter_dimension=1, tiled=True).astype(
-        jnp.bfloat16
+    parts = lax.axis_size("tensor")
+    pieces = lax.all_to_all(
+        partial_out.reshape(requests, parts, -1), "tensor", split_axis=1, concat_axis=1, tiled=True
     )
+    return jnp.sum(pieces, axis=1).astype(jnp.bfloat16)
 
 
 def solution(mesh):

time: 138 us -> 135 us (0.978)
  waiting for transfers between devices: 43 us -> 0.01 us
  blocking collectives: 0 us -> 41.9 us
  between operations: 13.7 us -> 0.37 us
  local copies, waits for them, and re-layouts: 29.1 us -> 41.2 us
    all_to_all x0 -> x1, blocking collectives: none -> 41.9 us  [body(): lax.all_to_all(partial_out.reshape(requests, parts, -1), 'tensor', split_...]
    reduce_scatter x1 -> x0, waiting for transfers between devices: 35.8 us -> none  [body(): lax.psum_scatter(partial_out, 'tensor', scatter_dimension=1, tiled=True)]
    dot_general x0 -> x1, local copies, waits for them, and re-layouts: none -> 12 us  [body(): partial_out = jnp.dot(attn, out_weight, preferred_element_type=jnp.float32)]
    all_to_all x1, waiting for transfers between devices: 7.14 us -> 0.01 us  [body(): lax.all_to_all(packed, 'group', split_axis=0, concat_axis=0, tiled=True)]
    convert_element_type x1 -> x0, other arithmetic: 1.7 us -> none  [body(): lax.psum_scatter(partial_out, 'tensor', scatter_dimension=1, tiled=True)]
  transfers between devices with their start and end apart: 3 -> 2, of which waited for: 2 -> 0; matrix products, arithmetic and copies ran while one was open for 22% -> 32% of each run, Pallas kernels for 0% -> 0%
where the time goes in v2:
time: 135 us; the launch traced here: 133 us
  blocking collectives  41.9 us (31%)
  local copies, waits for them, and re-layouts  41.2 us (31%)
  matrix products  33.2 us (25%)
  starting transfers between devices  8.46 us (6%)
  other arithmetic  7.58 us (6%)
    all_to_all x1, blocking collectives, body(): lax.all_to_all(partial_out.reshape(requests, parts, -1), 'tensor', split_...  41.9 us
    dot_general x1, local copies, waits for them, and re-layouts, body(): partial_out = jnp.dot(attn, out_weight, preferred_element_type=jnp.float32)  12 us
    gather x1, local copies, waits for them, and re-layouts, body(): far_keys = prefix_keys[block_table].reshape(local_groups, -1, width)  9.72 us
    gather x1, local copies, waits for them, and re-layouts, body(): far_values = prefix_values[block_table].reshape(local_groups, -1, width)  9.69 us
    dot_general x1, matrix products, body(): jnp.einsum('jqc,jtc->jqt', far_queries, far_keys, preferred_element_type=...  8.83 us
    dot_general x1, matrix products, body(): partial_out = jnp.dot(attn, out_weight, preferred_element_type=jnp.float32)  6.12 us
    dot_general x1, matrix products, body(): jnp.dot(hidden, query_weight, preferred_element_type=jnp.float32)  4.87 us
    dot_general x1, matrix products, body(): jnp.einsum('jqt,jtc->jqc', held_weights, far_values, preferred_element_ty...  4.8 us
  transfers between devices with their start and end apart: 2, of which 0 were waited for; matrix products, arithmetic and copies ran while one was open for 32% of the time, Pallas kernels for 0%

profile of v2, /device:TPU:2, one launch (start us, length us, event | category | flops | bytes accessed | tf_op | source)
XLA Modules:
  0.0 132.8 jit_solution(8343404605395643964)
XLA Ops:
  0.0 0.7 fusion.33
  1.2 4.9 %convolution_bitcast_fusion = f32[12,8,8,128]{3,1,2,0:T(8,128)S(1)} fusion(bf16[96,4096]{1,0:T(8,128)(2,1)S(1)} %copy-done, bf16[4096,1024]{1,0:T(8,128)(2,1)} %param.12), kind=kOutput, calls=%fused_computation.18 | convolution fusion | flops 805306368 | bytes 9568256 | tf_op jit(solution)/shard_map/dot_general | solution.py:83
  6.1 1.3 gather_fusion
  8.3 0.8 reshape.232
  9.1 4.3 %all-to-all-start = ((bf16[8,18,1024]{2,1,0:T(8,128)(2,1)}), bf16[8,18,1024]{2,1,0:T(8,128)(2,1)S(1)}, u32[]{:S(2)}, u32[]{:S(2)}) async-start(bf16[8,18,1024]{2,1,0:T(8,128)(2,1)} %reshape.232), calls=%async_computation | async-start | bytes 786432 | tf_op jit(solution)/shard_map/all_to_all | solution.py:94
  14.5 4.6 %fusion.45 = (f32[96,8]{1,0:T(8,128)S(1)}, f32[96,8,128]{2,1,0:T(8,128)S(1)}) fusion(bf16[96,128,256]{2,1,0:T(8,128)(2,1)} %param.19, bf16[96,8,256]{2,1,0:T(8,128)(2,1)S(1)} %mul.165, bf16[8,256]{1,0:T(8,128)(2,1)S(1)} %bitcast.75, pred[96,128]{1,0:T(8,128)(4,1)S(1)} %iota_compare_fusion.3), kind=kOutput, calls=%fused_computation.83 | convolution fusion | flops 50822400 | bytes 7097344 | tf_op jit(solution)/shard_map/rqc,rtc->rqt/dot_general | solution.py:146
  19.3 9.7 %gather_fusion.1 = bf16[1152,16,256]{2,1,0:T(8,128)(2,1)} fusion(bf16[1152,16,256]{2,1,0:T(8,128)(2,1)} %param.14, s32[2048]{0:T(1024)S(1)} %pad_clamp_fusion), kind=kCustom, calls=%fused_computation.1 | custom fusion | bytes 18878976 | tf_op jit(solution)/shard_map/gather | solution.py:107
  29.0 9.7 %gather_fusion.2 = bf16[1152,16,256]{2,1,0:T(8,128)(2,1)} fusion(bf16[1152,16,256]{2,1,0:T(8,128)(2,1)} %param.15, s32[2048]{0:T(1024)S(1)} %pad_clamp_fusion), kind=kCustom, calls=%fused_computation.2 | custom fusion | bytes 18878976 | tf_op jit(solution)/shard_map/gather | solution.py:108
  39.2 0.5 mul.156
  39.7 0.4 mul.157
  40.0 8.8 %fusion = (f32[18,64]{1,0:T(8,128)S(1)}, f32[18,64,1024]{2,1,0:T(8,128)}) fusion(pred[18,1024]{1,0:T(8,128)(4,1)S(1)} %iota_compare_fusion, bf16[18,1024,256]{2,1,0:T(8,128)(2,1)} %bitcast.56, bf16[18,64,256]{2,1,0:T(8,128)(2,1)S(1)} %mul.157, bf16[64,256]{1,0:T(8,128)(2,1)S(1)} %bitcast.71), kind=kOutput, calls=%fused_computation.6 | convolution fusion | flops 607812480 | bytes 14801408 | tf_op jit(solution)/shard_map/jqc,jtc->jqt/dot_general | solution.py:113
  49.0 4.0 %fusion.1 = f32[18,64]{1,0:T(8,128)S(1)} fusion(f32[18,64,1024]{2,1,0:T(8,128)} %get-tuple-element.23, f32[18,64]{1,0:T(8,128)S(1)} %get-tuple-element.22, pred[18,1024]{1,0:T(8,128)(4,1)S(1)} %iota_compare_fusion), kind=kLoop, calls=%fused_computation.7 | loop fusion | flops 5897088 | bytes 4746240 | tf_op jit(solution)/shard_map/reduce_sum | solution.py:32
  53.0 4.8 %fusion.3 = f32[18,64,256]{2,1,0:T(8,128)S(1)} fusion(bf16[18,1024,256]{2,1,0:T(8,128)(2,1)} %bitcast.58, f32[18,64,1024]{2,1,0:T(8,128)S(1)} %copy-done.3, f32[18,64]{1,0:T(8,128)S(1)} %get-tuple-element.22, pred[18,1024]{1,0:T(8,128)(4,1)S(1)} %iota_compare_fusion), kind=kOutput, calls=%fused_computation.9 | convolution fusion | flops 609878016 | bytes 15358464 | tf_op jit(solution)/shard_map/jqt,jtc->jqc/dot_general | solution.py:117
  57.8 0.6 reshape_reshape.4
  58.4 0.5 fusion.42
  59.5 1.1 copy.54
  60.6 4.2 %all-to-all-start.1 = ((f32[8,18,9,128]{3,1,2,0:T(8,128)}), f32[8,18,9,128]{3,1,2,0:T(8,128)S(1)}, u32[]{:S(2)}, u32[]{:S(2)}) async-start(f32[8,18,9,128]{3,1,2,0:T(8,128)} %copy.54), calls=%async_computation.1 | async-start | bytes 1769472 | tf_op jit(solution)/shard_map/all_to_all | solution.py:134
  64.8 3.8 %fusion.20 = f32[96,8,256]{2,1,0:T(8,128)S(1)} fusion(bf16[96,128,256]{2,1,0:T(8,128)(2,1)} %param.20, f32[96,8,128]{2,1,0:T(8,128)S(1)} %get-tuple-element.21, f32[96,8]{1,0:T(8,128)S(1)} %get-tuple-element.20, pred[96,128]{1,0:T(8,128)(4,1)S(1)} %iota_compare_fusion.3), kind=kOutput, calls=%fused_computation.37 | convolution fusion | flops 50626560 | bytes 7486464 | tf_op jit(solution)/shard_map/rqt,rtc->rqc/dot_general | solution.py:150
  68.6 0.4 reshape.239
  69.5 12.0 %copy.60 = bf16[4096,1024]{1,0:T(8,128)(2,1)} copy(bf16[4096,1024]{0,1:T(8,128)(2,1)} %bitcast.59) | data formatting | bytes 16777216 | tf_op jit(solution)/shard_map/dot_general | solution.py:156
  82.0 1.2 gather_fusion.3
  83.9 6.1 %fusion.46 = f32[96,4,1024]{2,0,1:T(8,128)S(1)} fusion(bf16[96,1024,1]{1,0,2:T(8,128)(2,1)S(1)} %reshape.290, bf16[4,1024,1024]{2,1,0:T(8,128)(2,1)} %bitcast.57), kind=kOutput, calls=%fused_computation.84 | convolution fusion | flops 805306368 | bytes 10158080 | tf_op jit(solution)/shard_map/dot_general | solution.py:156
  90.0 41.9 %all_to_all.15 = f32[96,4,1024]{2,0,1:T(8,128)S(1)} all-to-all(f32[96,4,1024]{2,0,1:T(8,128)S(1)} %fusion.46), channel_id=1, replica_groups=mesh['group'=8,'tensor'=4] {'tensor'}, dimensions={1} | all-to-all | bytes 3145728 | tf_op jit(solution)/shard_map/all_to_all | solution.py:158
  132.0 0.8 reduce_sum.29
  (59 shorter events, 5.3 us)
Async XLA Ops:
  0.0 1.1 copy-start
  1.2 5.0 %copy-start.2 = (s32[144]{0:T(256)S(1)}, s32[144]{0:T(256)}, u32[]{:S(2)}) copy-start(s32[144]{0:T(256)} %param.17) | copy-start | bytes 1732
  1.2 6.3 %copy-start.6 = (s32[96]{0:T(128)S(1)}, s32[96]{0:T(128)}, u32[]{:S(2)}) copy-start(s32[96]{0:T(128)} %param.21) | copy-start | bytes 1156
  1.2 6.9 %copy-start.5 = (s32[96]{0:T(128)S(1)}, s32[96]{0:T(128)}, u32[]{:S(2)}) copy-start(s32[96]{0:T(128)} %param.18) | copy-start | bytes 1156
  6.0 7.4 %copy-start.4 = (s32[18,64]{1,0:T(8,128)S(1)}, s32[18,64]{1,0:T(8,128)}, u32[]{:S(2)}) copy-start(s32[18,64]{1,0:T(8,128)} %param.16) | copy-start | bytes 13828
  9.1 29.7 %all-to-all-start = ((bf16[8,18,1024]{2,1,0:T(8,128)(2,1)}), bf16[8,18,1024]{2,1,0:T(8,128)(2,1)S(1)}, u32[]{:S(2)}, u32[]{:S(2)}) async-start(bf16[8,18,1024]{2,1,0:T(8,128)(2,1)} %reshape.232), calls=%async_computation | async-start | bytes 786432 | tf_op jit(solution)/shard_map/all_to_all | solution.py:94
  49.0 4.0 %copy-start.3 = (f32[18,64,1024]{2,1,0:T(8,128)S(1)}, f32[18,64,1024]{2,1,0:T(8,128)}, u32[]{:S(2)}) copy-start(f32[18,64,1024]{2,1,0:T(8,128)} %get-tuple-element.23) | copy-start | bytes 14155780
  60.6 21.2 %all-to-all-start.1 = ((f32[8,18,9,128]{3,1,2,0:T(8,128)}), f32[8,18,9,128]{3,1,2,0:T(8,128)S(1)}, u32[]{:S(2)}, u32[]{:S(2)}) async-start(f32[8,18,9,128]{3,1,2,0:T(8,128)} %copy.54), calls=%async_computation.1 | async-start | bytes 1769472 | tf_op jit(solution)/shard_map/all_to_all | solution.py:134
  83.9 48.9 %copy-start.1 = (bf16[96,4096]{1,0:T(8,128)(2,1)S(1)}, bf16[96,4096]{1,0:T(8,128)(2,1)}, u32[]{:S(2)}) copy-start(bf16[96,4096]{1,0:T(8,128)(2,1)} %param.11) | copy-start | bytes 2359300
